TPU v7x, 256 devices: a whole 4x4x8 slice. The times are simulated.
256 devices in a mesh: wide: 32 (over z, y), narrow: 8 (over x, core).
Axes of the slice: x: 4, y: 4, z: 8, core: 2. Of those that a mesh axis runs over, the one named last changes fastest.
Arguments:
- hidden: bfloat16 [65536, 8192], P('wide', 'narrow'), may hold values from -6 to 6
- base_key_value: bfloat16 [8192, 8, 2, 128], P('narrow'), may hold values from -0.0625 to 0.0625
- store_a: bfloat16 [256, 8192, 128], P('wide', 'narrow'), may hold values from -0.0625 to 0.0625
- stored_up_maps: bfloat16 [256, 2, 64, 8, 128], P('wide', None, None, 'narrow'), may hold values from -0.75 to 0.75
- adapter_ids: int32 [512], P('wide'), may hold values from 0 to 255, as said below
- span_start: int32 [512], P('wide'), may hold values from 0 to 31
Outputs:
- key_value: bfloat16 [8, 65536, 2, 128], P('narrow', 'wide')
Inputs may be any that keep to these rules, and one draw needn't show every extreme that they name: `adapter_ids`: requests of one replica that name different adapters name adapters of different owners, the owner of adapter a being the replica a // 8.
All inputs are finite; a program needn't handle non-finite values.
Results may differ from a plain program's by a relative error of at most 0.015.
Values may be sent and summed in bfloat16 or wider, within the bound.
No kernel may reach another device: no remote copies, remote signals or barrier semaphores. Data moves between devices by JAX's collectives and lax.ppermute only.
A program may use at most 192 MiB of HBM per device.

v0:
```python
import jax
import jax.numpy as jnp
from jax import lax
from jax.sharding import PartitionSpec as P

THETA = 500000.0


def rotate_keys(values, positions):
    half_dim = values.shape[-1] // 2
    frequency = THETA ** (-(jnp.arange(half_dim, dtype=jnp.float32) * 2.0 / values.shape[-1]))
    angles = positions[:, None] * frequency[None, :]
    angles = jnp.concatenate([angles, angles], axis=-1)
    turned = jnp.concatenate([-values[..., half_dim:], values[..., :half_dim]], axis=-1)
    return values * jnp.cos(angles) + turned * jnp.sin(angles)


def shards(hidden, base_key_value, store_a, stored_up_maps, adapter_ids, span_start):
    wide_count = lax.axis_size("wide")
    stored = store_a.shape[0]
    requests = adapter_ids.shape[0]
    span_len = hidden.shape[0] // requests
    rank_two = store_a.shape[2]
    owners = adapter_ids // stored
    slot_ids = adapter_ids % stored
    matches = owners[None, :] == jnp.arange(wide_count, dtype=jnp.int32)[:, None]
    wanted = jnp.max(jnp.where(matches, slot_ids[None, :] + 1, 0), axis=1).reshape(wide_count, 1)
    asked_slots = lax.all_to_all(wanted, "wide", split_axis=0, concat_axis=0, tiled=True)
    filled = asked_slots[:, 0] > 0
    chosen = jnp.maximum(asked_slots[:, 0] - 1, 0)
    reply_a = jnp.where(filled[:, None, None], store_a[chosen], jnp.zeros((), jnp.bfloat16))
    reply_b = jnp.where(
        filled[:, None, None, None, None], stored_up_maps[chosen], jnp.zeros((), jnp.bfloat16)
    )
    got_a, got_b = (
        lax.all_to_all(reply_a, "wide", split_axis=0, concat_axis=0, tiled=True),
        lax.all_to_all(reply_b, "wide", split_axis=0, concat_axis=0, tiled=True),
    )
    needed_a = got_a[owners]
    needed_b = got_b[owners]
    request_rows = hidden.reshape(requests, span_len, hidden.shape[1])
    shrink_part = jnp.einsum(
        "rtd,rdc->rtc", request_rows, needed_a, preferred_element_type=jnp.float32
    )
    shrunk = lax.psum(shrink_part.astype(jnp.bfloat16), "narrow")
    base_total_sum = lax.psum_scatter(
        jnp.einsum(
            "td,dhjc->htjc", hidden, base_key_value, preferred_element_type=jnp.float32
        ).astype(jnp.bfloat16),
        "narrow",
        scatter_dimension=0,
        tiled=True,
    ).astype(jnp.float32)
    rank = rank_two // 2
    shrunk_split = shrunk.reshape(requests, span_len, 2, rank)
    delta = jnp.einsum(
        "rtjk,rjkhc->hrtjc", shrunk_split, needed_b, preferred_element_type=jnp.float32
    )
    raw = base_total_sum + delta.reshape(base_total_sum.shape)
    positions = (
        (span_start[:, None] * span_len + jnp.arange(span_len, dtype=jnp.int32)[None, :])
        .reshape(-1)
        .astype(jnp.float32)
    )
    keys_turned = jax.vmap(lambda head_keys: rotate_keys(head_keys, positions))(raw[:, :, 0, :])
    joined = jnp.stack([keys_turned, raw[:, :, 1, :]], axis=2)
    return joined.astype(jnp.bfloat16)


def solution(mesh):
    placed = (
        P("wide", "narrow"),
        P("narrow", None, None, None),
        P("wide", "narrow", None),
        P("wide", None, None, "narrow", None),
        P("wide"),
        P("wide"),
    )
    return jax.shard_map(
        shards,
        mesh=mesh,
        in_specs=placed,
        out_specs=P("narrow", "wide", None, None),
        check_vma=False,
    )
```

profile of v0, /device:TPU:1, one launch (start us, length us, event | category | flops | bytes accessed | tf_op | source)
XLA Modules:
  0.0 383.8 jit_solution(11532929862729622991)
XLA Ops:
  6.5 0.0 copy-start
  6.5 0.8 compare_select_fusion
  7.4 0.1 select_reduce_fusion
  7.4 0.1 copy.22
  7.5 20.4 %all_to_all.19 = s32[32,1,1]{2,1,0:T(1,128)S(1)} all-to-all(s32[32,1,1]{2,1,0:T(1,128)S(1)} %copy.22), channel_id=1, replica_groups=mesh['wide'=32,'narrow'=8] {'wide'}, dimensions={0} | all-to-all | bytes 256 | tf_op jit(solution)/shard_map/all_to_all | solution.py:28
  28.0 0.7 maximum_reduce_fusion
  28.6 0.0 copy-done
  28.6 4.9 %gather_fusion.2 = bf16[32,1024,128]{2,1,0:T(8,128)(2,1)} fusion(bf16[8,1024,128]{2,1,0:T(8,128)(2,1)S(1)} %copy-done, s32[1024]{0:T(1024)S(1)} %pad_clamp_fusion.1), kind=kCustom, calls=%fused_computation.2 | custom fusion | bytes 16777344 | tf_op jit(solution)/shard_map/gather | solution.py:31
  33.5 0.7 compare_reduce_fusion
  34.2 7.2 %broadcast_select_fusion = bf16[32,1024,128]{2,1,0:T(8,128)(2,1)} fusion(bf16[32,1024,128]{2,1,0:T(8,128)(2,1)} %gather_fusion.2, pred[32]{0:T(512)(128)(4,1)S(1)} %compare_reduce_fusion), kind=kLoop, calls=%fused_computation.5 | loop fusion | flops 4194304 | bytes 16777248 | tf_op jit(solution)/shard_map/jit(_where)/select_n | solution.py:31
  41.4 5.0 %all-to-all-start.2 = ((bf16[32,1024,128]{2,1,0:T(8,128)(2,1)}), bf16[32,1024,128]{2,1,0:T(8,128)(2,1)}, u32[]{:S(2)}, u32[]{:S(2)}) async-start(bf16[32,1024,128]{2,1,0:T(8,128)(2,1)} %broadcast_select_fusion), calls=%async_computation.3 | async-start | bytes 16777216 | tf_op jit(solution)/shard_map/all_to_all | solution.py:36
  46.3 0.0 all-reduce.2.cloned.1.call-start
  46.4 189.5 %all-to-all-done.2 = bf16[32,1024,128]{2,1,0:T(8,128)(2,1)} async-done(((bf16[32,1024,128]{2,1,0:T(8,128)(2,1)}), bf16[32,1024,128]{2,1,0:T(8,128)(2,1)}, u32[]{:S(2)}, u32[]{:S(2)}) %all-to-all-start.2) | async-done | bytes 8388640 | tf_op jit(solution)/shard_map/all_to_all | solution.py:36
  235.9 6.4 %gather_fusion.3 = bf16[16,1024,128]{2,1,0:T(8,128)(2,1)} fusion(bf16[32,1024,128]{2,1,0:T(8,128)(2,1)} %all-to-all-done.2, s32[1024]{0:T(1024)S(1)} %pad_clamp_fusion), kind=kCustom, calls=%fused_computation.3 | custom fusion | bytes 8388672 | tf_op jit(solution)/shard_map/gather | solution.py:39
  242.4 5.8 %convolution_convert_fusion = bf16[16,128,128]{2,1,0:T(8,128)(2,1)} fusion(bf16[16,1024,128]{2,1,0:T(8,128)(2,1)} %gather_fusion.3, bf16[16,128,1024]{2,1,0:T(8,128)(2,1)} %bitcast.39), kind=kOutput, calls=%fused_computation.10 | convolution fusion | flops 537133056 | bytes 8912896 | tf_op jit(solution)/shard_map/rtd,rdc->rtc/dot_general | solution.py:42
  248.1 0.0 all-reduce.2.cloned.1.call-update
  248.1 0.0 reduce-scatter.2.cloned.1.call-start
  248.2 14.5 %convert_bitcast_fusion = bf16[8,2048,2,128]{1,3,2,0:T(8,128)(2,1)} fusion(bf16[2048,1024]{1,0:T(8,128)(2,1)} %param.6, bf16[1024,8,2,128]{3,2,1,0:T(2,128)(2,1)} %param.7), kind=kOutput, calls=%fused_computation.4 | convolution fusion | flops 8594128896 | bytes 16777216 | tf_op jit(solution)/shard_map/td,dhjc->htjc/dot_general | solution.py:47
  262.7 0.0 copy-start.2
  262.7 0.0 reduce-scatter.2.cloned.1.call-update
  262.7 0.0 copy-start.3
  262.7 0.9 copy-done.2
  263.6 0.7 gather_fusion
  264.4 1.1 bitcast_select_fusion
  265.5 5.8 %all-to-all-start.1 = ((bf16[32,2,64,1,128]{4,2,1,3,0:T(8,128)(2,1)}), bf16[32,2,64,1,128]{4,2,1,3,0:T(8,128)(2,1)S(1)}, u32[]{:S(2)}, u32[]{:S(2)}) async-start(bf16[32,2,64,1,128]{4,2,1,3,0:T(8,128)(2,1)} %bitcast_select_fusion), calls=%async_computation.2 | async-start | bytes 2097152 | tf_op jit(solution)/shard_map/all_to_all | solution.py:37
  271.3 0.0 copy-done.3
  271.3 0.1 convert_bitcast_fusion.1
  271.4 0.1 multiply_bitcast_fusion
  271.5 25.2 %all-to-all-done.1 = bf16[32,2,64,1,128]{4,2,1,3,0:T(8,128)(2,1)S(1)} async-done(((bf16[32,2,64,1,128]{4,2,1,3,0:T(8,128)(2,1)}), bf16[32,2,64,1,128]{4,2,1,3,0:T(8,128)(2,1)S(1)}, u32[]{:S(2)}, u32[]{:S(2)}) %all-to-all-start.1) | async-done | bytes 1048608 | tf_op jit(solution)/shard_map/all_to_all | solution.py:37
  296.7 0.6 gather_fusion.1
  297.3 13.9 %all-reduce.2.cloned.1.call-done = bf16[16,128,2,64]{1,3,2,0:T(8,128)(2,1)} async-done(((bf16[16,128,2,64]{1,3,2,0:T(8,128)(2,1)}), bf16[16,128,2,64]{1,3,2,0:T(8,128)(2,1)}) %all-reduce.2.cloned.1.call-update) | async-done | bytes 524304 | tf_op jit(solution)/shard_map/psum | solution.py:45
  311.2 1.5 convolution_bitcast_fusion
  312.7 2.0 copy.24
  314.7 1.7 reshape.278
  316.4 52.8 %reduce-scatter.2.cloned.1.call-done = bf16[1,2048,2,128]{1,3,2,0:T(8,128)(2,1)} async-done(((bf16[8,2048,2,128]{1,3,2,0:T(8,128)(2,1)}), bf16[1,2048,2,128]{1,3,2,0:T(8,128)(2,1)}) %reduce-scatter.2.cloned.1.call-update) | async-done | bytes 1048592 | tf_op jit(solution)/shard_map/reduce_scatter | solution.py:46
  369.2 1.5 convert_add_fusion
  370.7 0.1 slice_bitcast_fusion
  370.8 0.1 slice.36
  370.9 0.0 copy-start.1
  370.9 0.1 fusion.8
  371.0 3.9 %fusion.6 = bf16[1,2048,1,128]{1,3,2,0:T(8,128)(2,1)S(1)} fusion(f32[1,2048,1,64]{1,3,2,0:T(8,128)S(1)} %multiply_bitcast_fusion, f32[1,2048,1,64]{1,3,2,0:T(8,128)S(1)} %get-tuple-element.8, f32[1,2048,1,64]{1,3,2,0:T(8,128)S(1)} %get-tuple-element.7, f32[1,2048,2,128]{1,3,2,0:T(8,128)S(1)} %convert_add_fusion), kind=kLoop, calls=%fused_computation.17 | loop fusion | flops 1572864 | bytes 3145728 | tf_op jit(solution)/shard_map/convert
  374.8 0.1 pad_maximum_fusion.1
  374.9 2.0 copy.25
  376.9 0.0 copy-done.1
  (4 shorter events, 0.0 us)
Async XLA Ops:
  6.5 22.1 %copy-start = (bf16[8,1024,128]{2,1,0:T(8,128)(2,1)S(1)}, bf16[8,1024,128]{2,1,0:T(8,128)(2,1)}, u32[]{:S(2)}) copy-start(bf16[8,1024,128]{2,1,0:T(8,128)(2,1)} %param.8) | copy-start | bytes 6291460
  41.4 194.5 %all-to-all-start.2 = ((bf16[32,1024,128]{2,1,0:T(8,128)(2,1)}), bf16[32,1024,128]{2,1,0:T(8,128)(2,1)}, u32[]{:S(2)}, u32[]{:S(2)}) async-start(bf16[32,1024,128]{2,1,0:T(8,128)(2,1)} %broadcast_select_fusion), calls=%async_computation.3 | async-start | bytes 16777216 | tf_op jit(solution)/shard_map/all_to_all | solution.py:36
  46.3 264.8 %all-reduce.2.cloned.1.call-start = ((), (), s32[]{:S(2)}) async-start(), calls=%async_computation.5 | async-start | bytes 1048576 | tf_op jit(solution)/shard_map/psum | solution.py:45
  248.1 121.1 %reduce-scatter.2.cloned.1.call-start = ((), (), s32[]{:S(2)}) async-start(), calls=%async_computation.4 | async-start | bytes 9437184 | tf_op jit(solution)/shard_map/reduce_scatter | solution.py:46
  262.7 1.0 copy-start.2
  262.7 8.6 %copy-start.3 = (s32[16]{0:T(128)S(1)}, s32[16]{0:T(128)}, u32[]{:S(2)}) copy-start(s32[16]{0:T(128)} %param.11) | copy-start | bytes 196
  265.5 31.2 %all-to-all-start.1 = ((bf16[32,2,64,1,128]{4,2,1,3,0:T(8,128)(2,1)}), bf16[32,2,64,1,128]{4,2,1,3,0:T(8,128)(2,1)S(1)}, u32[]{:S(2)}, u32[]{:S(2)}) async-start(bf16[32,2,64,1,128]{4,2,1,3,0:T(8,128)(2,1)} %bitcast_select_fusion), calls=%async_computation.2 | async-start | bytes 2097152 | tf_op jit(solution)/shard_map/all_to_all | solution.py:37
  370.9 6.1 %copy-start.1 = (bf16[8,1024,128]{2,1,0:T(8,128)(2,1)S(1)}, bf16[8,1024,128]{2,1,0:T(8,128)(2,1)}, u32[]{:S(2)}) copy-start(bf16[8,1024,128]{2,1,0:T(8,128)(2,1)} %param.8) | copy-start | bytes 6291460
Sparse Core Ops, SparseCore 0:
  248.3 62.8 all-reduce.1
  313.7 55.4 reduce-scatter.1
where the time goes:
time: 384 us
  waiting for transfers between devices  281 us (73%)
  matrix products  21.8 us (6%)
  blocking collectives  20.4 us (5%)
  local copies, waits for them, and re-layouts  19.5 us (5%)
  other arithmetic  16.3 us (4%)
  between operations  13.6 us (4%)
  starting transfers between devices  10.8 us (3%)
    all_to_all x1, waiting for transfers between devices, shards(): lax.all_to_all(reply_a, 'wide', split_axis=0, concat_axis=0, tiled=True)  190 us
    reduce_scatter x1, waiting for transfers between devices, shards(): lax.psum_scatter(jnp.einsum('td,dhjc->htjc', hidden, base_key_value, pref...  52.8 us
    all_to_all x1, waiting for transfers between devices, shards(): lax.all_to_all(reply_b, 'wide', split_axis=0, concat_axis=0, tiled=True)  25.2 us
    all_to_all x1, blocking collectives, shards(): lax.all_to_all(wanted, 'wide', split_axis=0, concat_axis=0, tiled=True)  20.4 us
    dot_general x1, matrix products, shards(): jnp.einsum('td,dhjc->htjc', hidden, base_key_value, preferred_element_typ...  14.5 us
    psum x1, waiting for transfers between devices, shards(): shrunk = lax.psum(shrink_part.astype(jnp.bfloat16), 'narrow')  13.9 us
  transfers between devices with their start and end apart: 4, of which 4 were waited for; matrix products, arithmetic and copies ran while one was open for 6% of the time, Pallas kernels for 0%

commit v1 on v0

--- a/solution.py
+++ b/solution.py
@@ -42,7 +42,7 @@
     shrink_part = jnp.einsum(
         "rtd,rdc->rtc", request_rows, needed_a, preferred_element_type=jnp.float32
     )
-    shrunk = lax.psum(shrink_part.astype(jnp.bfloat16), "narrow")
+    shrunk = jnp.sum(lax.all_gather(shrink_part.astype(jnp.bfloat16), "narrow"), axis=0)
     base_total_sum = lax.psum_scatter(
         jnp.einsum(
             "td,dhjc->htjc", hidden, base_key_value, preferred_element_type=jnp.float32

time: 384 us -> 354 us (0.922)
  waiting for transfers between devices: 281 us -> 246 us
    reduce_scatter x1, waiting for transfers between devices: 52.8 us -> 31.6 us  [shards(): lax.psum_scatter(jnp.einsum('td,dhjc->htjc', hidden, base_key_value, pref...]
    psum x1 -> x0, waiting for transfers between devices: 13.9 us -> none  [shards(): shrunk = lax.psum(shrink_part.astype(jnp.bfloat16), 'narrow')]
  transfers between devices with their start and end apart: 4 -> 4, of which waited for: 4 -> 3; matrix products, arithmetic and copies ran while one was open for 6% -> 7% of each run, Pallas kernels for 0% -> 0%
where the time goes in v1:
time: 354 us; the launch traced here: 353 us
  waiting for transfers between devices  246 us (69%)
  local copies, waits for them, and re-layouts  21.6 us (6%)
  matrix products  21 us (6%)
  blocking collectives  20.4 us (6%)
  other arithmetic  19.3 us (5%)
  between operations  13.6 us (4%)
  starting transfers between devices  10.8 us (3%)
    all_to_all x1, waiting for transfers between devices, shards(): lax.all_to_all(reply_a, 'wide', split_axis=0, concat_axis=0, tiled=True)  190 us
    reduce_scatter x1, waiting for transfers between devices, shards(): lax.psum_scatter(jnp.einsum('td,dhjc->htjc', hidden, base_key_value, pref...  31.6 us
    all_to_all x1, waiting for transfers between devices, shards(): lax.all_to_all(reply_b, 'wide', split_axis=0, concat_axis=0, tiled=True)  25.2 us
    all_to_all x1, blocking collectives, shards(): lax.all_to_all(wanted, 'wide', split_axis=0, concat_axis=0, tiled=True)  20.4 us
    dot_general x1, matrix products, shards(): jnp.einsum('td,dhjc->htjc', hidden, base_key_value, preferred_element_typ...  14.5 us
    select_n x1, other arithmetic, shards(): jnp.where(filled[:, None, None], store_a[chosen], jnp.zeros((), jnp.bfloa...  7.22 us
  transfers between devices with their start and end apart: 4, of which 3 were waited for; matrix products, arithmetic and copies ran while one was open for 7% of the time, Pallas kernels for 0%

profile of v1, /device:TPU:1, one launch (start us, length us, event | category | flops | bytes accessed | tf_op | source)
XLA Modules:
  0.0 353.0 jit_solution(9496316345119658377)
XLA Ops:
  6.5 0.0 copy-start
  6.5 0.8 compare_select_fusion
  7.4 0.1 select_reduce_fusion
  7.4 0.1 copy.38
  7.5 20.4 %all_to_all.19 = s32[32,1,1]{2,1,0:T(1,128)S(1)} all-to-all(s32[32,1,1]{2,1,0:T(1,128)S(1)} %copy.38), channel_id=1, replica_groups=mesh['wide'=32,'narrow'=8] {'wide'}, dimensions={0} | all-to-all | bytes 256 | tf_op jit(solution)/shard_map/all_to_all | solution.py:28
  28.0 0.7 maximum_reduce_fusion
  28.6 0.0 copy-done
  28.6 4.9 %gather_fusion.2 = bf16[32,1024,128]{2,1,0:T(8,128)(2,1)} fusion(bf16[8,1024,128]{2,1,0:T(8,128)(2,1)S(1)} %copy-done, s32[1024]{0:T(1024)S(1)} %pad_clamp_fusion.1), kind=kCustom, calls=%fused_computation.2 | custom fusion | bytes 16777344 | tf_op jit(solution)/shard_map/gather | solution.py:31
  33.5 0.7 compare_reduce_fusion
  34.2 7.2 %broadcast_select_fusion = bf16[32,1024,128]{2,1,0:T(8,128)(2,1)} fusion(bf16[32,1024,128]{2,1,0:T(8,128)(2,1)} %gather_fusion.2, pred[32]{0:T(512)(128)(4,1)S(1)} %compare_reduce_fusion), kind=kLoop, calls=%fused_computation.5 | loop fusion | flops 4194304 | bytes 16777248 | tf_op jit(solution)/shard_map/jit(_where)/select_n | solution.py:31
  41.4 5.0 %all-to-all-start.2 = ((bf16[32,1024,128]{2,1,0:T(8,128)(2,1)}), bf16[32,1024,128]{2,1,0:T(8,128)(2,1)}, u32[]{:S(2)}, u32[]{:S(2)}) async-start(bf16[32,1024,128]{2,1,0:T(8,128)(2,1)} %broadcast_select_fusion), calls=%async_computation.3 | async-start | bytes 16777216 | tf_op jit(solution)/shard_map/all_to_all | solution.py:36
  46.3 0.0 all-gather.3.cloned.1.call-start
  46.4 189.5 %all-to-all-done.2 = bf16[32,1024,128]{2,1,0:T(8,128)(2,1)} async-done(((bf16[32,1024,128]{2,1,0:T(8,128)(2,1)}), bf16[32,1024,128]{2,1,0:T(8,128)(2,1)}, u32[]{:S(2)}, u32[]{:S(2)}) %all-to-all-start.2) | async-done | bytes 8388640 | tf_op jit(solution)/shard_map/all_to_all | solution.py:36
  235.9 6.4 %gather_fusion.3 = bf16[16,1024,128]{2,1,0:T(8,128)(2,1)} fusion(bf16[32,1024,128]{2,1,0:T(8,128)(2,1)} %all-to-all-done.2, s32[1024]{0:T(1024)S(1)} %pad_clamp_fusion), kind=kCustom, calls=%fused_computation.3 | custom fusion | bytes 8388672 | tf_op jit(solution)/shard_map/gather | solution.py:39
  242.4 4.9 %fusion.2 = bf16[16,128,128]{1,2,0:T(8,128)(2,1)S(1)} fusion(bf16[16,1024,128]{2,1,0:T(8,128)(2,1)} %gather_fusion.3, bf16[16,128,1024]{2,1,0:T(8,128)(2,1)} %bitcast.41), kind=kOutput, calls=%fused_computation.11 | convolution fusion | flops 537133056 | bytes 8912896 | tf_op jit(solution)/shard_map/rtd,rdc->rtc/dot_general | solution.py:42
  247.3 1.0 copy.40
  248.3 0.0 all-gather.3.cloned.1.call-update
  248.3 0.0 reduce-scatter.2.cloned.1.call-start
  248.4 14.5 %convert_bitcast_fusion = bf16[8,2048,2,128]{1,3,2,0:T(8,128)(2,1)} fusion(bf16[2048,1024]{1,0:T(8,128)(2,1)} %param.6, bf16[1024,8,2,128]{3,2,1,0:T(2,128)(2,1)} %param.7), kind=kOutput, calls=%fused_computation.4 | convolution fusion | flops 8594128896 | bytes 16777216 | tf_op jit(solution)/shard_map/td,dhjc->htjc/dot_general | solution.py:47
  262.8 0.0 copy-start.2
  262.8 0.0 reduce-scatter.2.cloned.1.call-update
  262.9 0.0 copy-start.3
  262.9 0.9 copy-done.2
  263.8 0.7 gather_fusion
  264.6 1.1 bitcast_select_fusion
  265.7 5.8 %all-to-all-start.1 = ((bf16[32,2,64,1,128]{4,2,1,3,0:T(8,128)(2,1)}), bf16[32,2,64,1,128]{4,2,1,3,0:T(8,128)(2,1)S(1)}, u32[]{:S(2)}, u32[]{:S(2)}) async-start(bf16[32,2,64,1,128]{4,2,1,3,0:T(8,128)(2,1)} %bitcast_select_fusion), calls=%async_computation.2 | async-start | bytes 2097152 | tf_op jit(solution)/shard_map/all_to_all | solution.py:37
  271.5 0.0 copy-done.3
  271.5 0.1 convert_bitcast_fusion.1
  271.6 0.1 multiply_bitcast_fusion
  271.7 25.2 %all-to-all-done.1 = bf16[32,2,64,1,128]{4,2,1,3,0:T(8,128)(2,1)S(1)} async-done(((bf16[32,2,64,1,128]{4,2,1,3,0:T(8,128)(2,1)}), bf16[32,2,64,1,128]{4,2,1,3,0:T(8,128)(2,1)S(1)}, u32[]{:S(2)}, u32[]{:S(2)}) %all-to-all-start.1) | async-done | bytes 1048608 | tf_op jit(solution)/shard_map/all_to_all | solution.py:37
  296.9 1.4 gather_fusion.1
  298.3 0.0 all-gather.3.cloned.1.call-done
  298.3 3.0 reduce_sum.12
  301.2 0.3 copy.41
  301.5 1.5 convolution_bitcast_fusion
  303.1 2.0 copy.42
  305.0 1.8 reshape.278
  306.8 31.6 %reduce-scatter.2.cloned.1.call-done = bf16[1,2048,2,128]{1,3,2,0:T(8,128)(2,1)} async-done(((bf16[8,2048,2,128]{1,3,2,0:T(8,128)(2,1)}), bf16[1,2048,2,128]{1,3,2,0:T(8,128)(2,1)}) %reduce-scatter.2.cloned.1.call-update) | async-done | bytes 1048592 | tf_op jit(solution)/shard_map/reduce_scatter | solution.py:46
  338.4 1.5 convert_add_fusion
  339.9 0.1 slice_bitcast_fusion
  340.0 0.1 slice.36
  340.1 0.0 copy-start.1
  340.1 0.1 fusion.9
  340.2 3.9 %fusion.7 = bf16[1,2048,1,128]{1,3,2,0:T(8,128)(2,1)S(1)} fusion(f32[1,2048,1,64]{1,3,2,0:T(8,128)S(1)} %multiply_bitcast_fusion, f32[1,2048,1,64]{1,3,2,0:T(8,128)S(1)} %get-tuple-element.8, f32[1,2048,1,64]{1,3,2,0:T(8,128)S(1)} %get-tuple-element.7, f32[1,2048,2,128]{1,3,2,0:T(8,128)S(1)} %convert_add_fusion), kind=kLoop, calls=%fused_computation.18 | loop fusion | flops 1572864 | bytes 3145728 | tf_op jit(solution)/shard_map/convert.1
  344.1 0.1 pad_maximum_fusion.1
  344.2 2.0 copy.43
  346.2 0.0 copy-done.1
  (4 shorter events, 0.0 us)
Async XLA Ops:
  6.5 22.1 %copy-start = (bf16[8,1024,128]{2,1,0:T(8,128)(2,1)S(1)}, bf16[8,1024,128]{2,1,0:T(8,128)(2,1)}, u32[]{:S(2)}) copy-start(bf16[8,1024,128]{2,1,0:T(8,128)(2,1)} %param.8) | copy-start | bytes 6291460
  41.4 194.5 %all-to-all-start.2 = ((bf16[32,1024,128]{2,1,0:T(8,128)(2,1)}), bf16[32,1024,128]{2,1,0:T(8,128)(2,1)}, u32[]{:S(2)}, u32[]{:S(2)}) async-start(bf16[32,1024,128]{2,1,0:T(8,128)(2,1)} %broadcast_select_fusion), calls=%async_computation.3 | async-start | bytes 16777216 | tf_op jit(solution)/shard_map/all_to_all | solution.py:36
  46.3 251.9 %all-gather.3.cloned.1.call-start = ((), (), s32[]{:S(2)}) async-start(), calls=%async_computation.5 | async-start | bytes 4718592 | tf_op jit(solution)/shard_map/all_gather | solution.py:45
  248.3 90.1 %reduce-scatter.2.cloned.1.call-start = ((), (), s32[]{:S(2)}) async-start(), calls=%async_computation.4 | async-start | bytes 9437184 | tf_op jit(solution)/shard_map/reduce_scatter | solution.py:46
  262.8 0.9 copy-start.2
  262.9 8.6 %copy-start.3 = (s32[16]{0:T(128)S(1)}, s32[16]{0:T(128)}, u32[]{:S(2)}) copy-start(s32[16]{0:T(128)} %param.11) | copy-start | bytes 196
  265.7 31.2 %all-to-all-start.1 = ((bf16[32,2,64,1,128]{4,2,1,3,0:T(8,128)(2,1)}), bf16[32,2,64,1,128]{4,2,1,3,0:T(8,128)(2,1)S(1)}, u32[]{:S(2)}, u32[]{:S(2)}) async-start(bf16[32,2,64,1,128]{4,2,1,3,0:T(8,128)(2,1)} %bitcast_select_fusion), calls=%async_computation.2 | async-start | bytes 2097152 | tf_op jit(solution)/shard_map/all_to_all | solution.py:37
  340.1 6.1 %copy-start.1 = (bf16[8,1024,128]{2,1,0:T(8,128)(2,1)S(1)}, bf16[8,1024,128]{2,1,0:T(8,128)(2,1)}, u32[]{:S(2)}) copy-start(bf16[8,1024,128]{2,1,0:T(8,128)(2,1)} %param.8) | copy-start | bytes 6291460
Sparse Core Ops, SparseCore 0:
  248.4 33.3 all-gather.2
  284.3 54.0 reduce-scatter.1
